TPU v7x, 512 devices: a whole 4x8x8 slice. The times are simulated.
512 devices in a mesh: ctx: 64 (over z_hi, y, core), head: 8 (over x, z_lo).
Axes of the slice: x: 4, y: 8, z: 8 (z_hi: 4, z_lo: 2; z = z_hi * 2 + z_lo), core: 2. Of those that a mesh axis runs over, the one named last changes fastest.
Arguments:
- queries: bfloat16 [65536, 8192], P(('ctx', 'head')), may hold values from -13 to 13
- keys: bfloat16 [65536, 1024], P(('ctx', 'head')), may hold values from -13 to 13
- values: bfloat16 [65536, 1024], P(('ctx', 'head')), may hold values from -6 to 6
- doc_ids: int32 [65536], replicated, may hold values from 0 to 63, never falling along the last dimension, each value on 1 to 1280 neighbouring positions
Outputs:
- attended: bfloat16 [65536, 8192], P(('ctx', 'head'))
Inputs may be any that keep to these rules, and one draw needn't show every extreme that they name: `doc_ids`: document numbers never fall along the sequence; every document has 1 to 1280 tokens and one has exactly 1280; every number of 0 to 63 occurs.
All inputs are finite; a program needn't handle non-finite values.
Results may differ from a plain program's by a relative error of at most 0.0025.
Values may be sent and summed in bfloat16 or wider, within the bound.
No kernel may reach another device: no remote copies, remote signals or barrier semaphores. Data moves between devices by JAX's collectives and lax.ppermute only.
A program may use at most 64 MiB of HBM per device.

v0:
```python
import jax
import jax.numpy as jnp
from jax import lax
from jax.sharding import PartitionSpec as P

HD = 128
QH = 64
KVH = 8
BLOCK = 256
DOC_BLOCKS = 5
QBLK_DEV = 4
PREV = 2
floor_score = -1e30


def from_behind(value, axis, steps):
    count = lax.axis_size(axis)
    leading, last = (max(0, -steps), min(count, count - steps))
    return lax.ppermute(value, axis, [(source, source + steps) for source in range(leading, last)])


def attend_tile(running, query_block, key_tile, value_tile, allowed):
    maxima, totals, accum = running
    scores = jnp.einsum(
        "qgjd,kgd->qgjk", query_block, key_tile, preferred_element_type=jnp.float32
    ) * HD ** (-0.5)
    scores = jnp.where(allowed[:, None, None, :], scores, floor_score)
    fresh = jnp.maximum(maxima, jnp.max(scores, axis=-1))
    factor = jnp.exp(maxima - fresh)
    weights = jnp.exp(scores - fresh[..., None])
    totals = totals * factor + jnp.sum(weights, axis=-1)
    accum = accum * factor[..., None] + jnp.einsum(
        "qgjk,kgd->qgjd",
        weights.astype(jnp.bfloat16),
        value_tile,
        preferred_element_type=jnp.float32,
    )
    return (fresh, totals, accum)


def key_window(paired):
    pieces = []
    for offset in range(1, PREV + 1):
        pieces.append(from_behind(paired, "ctx", offset))
    return jnp.concatenate(pieces[::-1] + [paired], axis=1)


def shards(queries, keys, values, doc_ids):
    per_group = QH // KVH
    range_rows = QBLK_DEV * BLOCK
    ctx_pos = lax.axis_index("ctx")
    local_queries, local_keys, local_values = (
        lax.all_to_all(queries, "head", split_axis=1, concat_axis=0, tiled=True),
        lax.all_to_all(keys, "head", split_axis=1, concat_axis=0, tiled=True),
        lax.all_to_all(values, "head", split_axis=1, concat_axis=0, tiled=True),
    )
    window = key_window(jnp.stack([local_keys, local_values]))
    groups = local_keys.shape[1] // HD
    window_keys = window[0].reshape(-1, groups, HD)
    window_values = window[1].reshape(-1, groups, HD)
    padded_ids = jnp.concatenate([jnp.full((PREV * range_rows,), -1, jnp.int32), doc_ids])
    window_ids = lax.dynamic_slice_in_dim(padded_ids, ctx_pos * range_rows, (PREV + 1) * range_rows)
    range_ids = lax.dynamic_slice_in_dim(doc_ids, ctx_pos * range_rows, range_rows)
    window_base = (ctx_pos - PREV) * range_rows
    offsets = jnp.arange(BLOCK, dtype=jnp.int32)
    shaped_queries = local_queries.reshape(range_rows, groups, per_group, HD)
    outputs = []
    for block_index in range(QBLK_DEV):
        query_block = shaped_queries[block_index * BLOCK : (block_index + 1) * BLOCK]
        block_ids = range_ids[block_index * BLOCK : (block_index + 1) * BLOCK]
        query_pos = ctx_pos * range_rows + block_index * BLOCK + offsets

        def visit(running, tile, query_block=query_block, block_ids=block_ids, query_pos=query_pos):
            start = tile * BLOCK
            key_tile = lax.dynamic_slice_in_dim(window_keys, start, BLOCK, 0)
            value_tile = lax.dynamic_slice_in_dim(window_values, start, BLOCK, 0)
            tile_ids = lax.dynamic_slice_in_dim(window_ids, start, BLOCK)
            key_pos = window_base + start + offsets
            allowed = (block_ids[:, None] == tile_ids[None, :]) & (
                key_pos[None, :] <= query_pos[:, None]
            )
            return attend_tile(running, query_block, key_tile, value_tile, allowed)

        initial = (
            jnp.full((BLOCK, groups, per_group), floor_score, jnp.float32),
            jnp.zeros((BLOCK, groups, per_group), jnp.float32),
            jnp.zeros((BLOCK, groups, per_group, HD), jnp.float32),
        )
        diagonal = PREV * QBLK_DEV + block_index
        running = visit(initial, diagonal)

        def backward(offset, running, visit=visit, block_ids=block_ids, diagonal=diagonal):
            tile = diagonal - offset
            return visit(running, tile)

        running = lax.fori_loop(1, DOC_BLOCKS + 1, backward, running)
        maxima, totals, accum = running
        outputs.append(
            (accum / totals[..., None]).astype(jnp.bfloat16).reshape(BLOCK, groups * per_group * HD)
        )
    local_out = jnp.concatenate(outputs, axis=0)
    return lax.all_to_all(local_out, "head", split_axis=0, concat_axis=1, tiled=True)


def solution(mesh):
    in_specs = (P(("ctx", "head"), None), P(("ctx", "head"), None), P(("ctx", "head"), None), P())
    out_specs = P(("ctx", "head"), None)
    return jax.shard_map(shards, mesh=mesh, in_specs=in_specs, out_specs=out_specs, check_vma=False)
```

profile of v0, /device:TPU:128, one launch (start us, length us, event | category | flops | bytes accessed | tf_op | source)
XLA Modules:
  0.0 223.2 jit_solution(8170471879626285882)
XLA Ops:
  1.7 6.1 %all-to-all-start = ((bf16[128,8,128]{2,0,1:T(8,128)(2,1)}), bf16[128,8,128]{2,0,1:T(8,128)(2,1)S(1)}, u32[]{:S(2)}, u32[]{:S(2)}) async-start(bf16[128,8,128]{2,0,1:T(8,128)(2,1)} %copy_bitcast_fusion.2), calls=%async_computation | async-start | bytes 524288 | tf_op jit(solution)/shard_map/all_to_all | solution.py:54
  7.8 1.7 copy_bitcast_fusion.1
  9.5 5.6 %all-to-all-done = bf16[128,8,128]{2,0,1:T(8,128)(2,1)S(1)} async-done(((bf16[128,8,128]{2,0,1:T(8,128)(2,1)}), bf16[128,8,128]{2,0,1:T(8,128)(2,1)S(1)}, u32[]{:S(2)}, u32[]{:S(2)}) %all-to-all-start) | async-done | bytes 262176 | tf_op jit(solution)/shard_map/all_to_all | solution.py:54
  15.1 3.4 %all-to-all-start.2 = ((bf16[128,8,128]{2,0,1:T(8,128)(2,1)}), bf16[128,8,128]{2,0,1:T(8,128)(2,1)S(1)}, u32[]{:S(2)}, u32[]{:S(2)}) async-start(bf16[128,8,128]{2,0,1:T(8,128)(2,1)} %copy_bitcast_fusion.1), calls=%async_computation.2 | async-start | bytes 524288 | tf_op jit(solution)/shard_map/all_to_all | solution.py:55
  18.5 1.6 copy.129
  20.1 5.7 %all-to-all-done.2 = bf16[128,8,128]{2,0,1:T(8,128)(2,1)S(1)} async-done(((bf16[128,8,128]{2,0,1:T(8,128)(2,1)}), bf16[128,8,128]{2,0,1:T(8,128)(2,1)S(1)}, u32[]{:S(2)}, u32[]{:S(2)}) %all-to-all-start.2) | async-done | bytes 262176 | tf_op jit(solution)/shard_map/all_to_all | solution.py:55
  25.7 3.7 %all-to-all-start.1 = ((bf16[128,8,1024]{2,0,1:T(8,128)(2,1)}), bf16[128,8,1024]{2,0,1:T(8,128)(2,1)S(1)}, u32[]{:S(2)}, u32[]{:S(2)}) async-start(bf16[128,8,1024]{2,0,1:T(8,128)(2,1)} %bitcast.405), calls=%async_computation.1 | async-start | bytes 4194304 | tf_op jit(solution)/shard_map/all_to_all | solution.py:53
  30.4 3.5 %collective-permute-start = (bf16[2,1024,128]{2,1,0:T(8,128)(2,1)S(1)}, bf16[2,1024,128]{2,1,0:T(8,128)(2,1)S(1)}, u32[]{:S(2)}, u32[]{:S(2)}) collective-permute-start(bf16[2,1024,128]{2,1,0:T(8,128)(2,1)S(1)} %pad_maximum_fusion.1), channel_id=1, source_target_pairs={{0,16},{8,24},{16,32},{24,40},{32,48},{40,56},{48,64},{56,72},{64,... | collective-permute-start | bytes 1572872 | tf_op jit(solution)/shard_map/ppermute | solution.py:19
  33.9 1.9 collective-permute-start.1
  36.9 28.3 %collective-permute-done = bf16[2,1024,128]{2,1,0:T(8,128)(2,1)S(1)} collective-permute-done((bf16[2,1024,128]{2,1,0:T(8,128)(2,1)S(1)}, bf16[2,1024,128]{2,1,0:T(8,128)(2,1)S(1)}, u32[]{:S(2)}, u32[]{:S(2)}) %collective-permute-start) | collective-permute-done | bytes 524320 | tf_op jit(solution)/shard_map/ppermute | solution.py:19
  65.2 3.8 %collective-permute-done.1 = bf16[2,1024,128]{2,1,0:T(8,128)(2,1)S(1)} collective-permute-done((bf16[2,1024,128]{2,1,0:T(8,128)(2,1)S(1)}, bf16[2,1024,128]{2,1,0:T(8,128)(2,1)S(1)}, u32[]{:S(2)}, u32[]{:S(2)}) %collective-permute-start.1) | collective-permute-done | bytes 524320 | tf_op jit(solution)/shard_map/ppermute | solution.py:19
  71.8 11.9 %all-to-all-done.1 = bf16[128,8,1024]{2,0,1:T(8,128)(2,1)S(1)} async-done(((bf16[128,8,1024]{2,0,1:T(8,128)(2,1)}), bf16[128,8,1024]{2,0,1:T(8,128)(2,1)S(1)}, u32[]{:S(2)}, u32[]{:S(2)}) %all-to-all-start.1) | async-done | bytes 2097184 | tf_op jit(solution)/shard_map/all_to_all | solution.py:53
  85.8 2.5 %fusion.81 = f32[256,1,8,128]{3,0,2,1:T(8,128)} fusion(f32[256,1,8,256]{0,3,2,1:T(8,128)S(1)} %get-tuple-element.1194, f32[256,8]{0,1:T(8,128)S(1)} %get-tuple-element.1173, f32[256,8]{0,1:T(8,128)S(1)} %get-tuple-element.1171, bf16[1,1024,128]{2,1,0:T(8,128)(2,1)} %bitcast.433), kind=kOutput, calls=%fused_computation.120 | convolution fusion | flops 135528448 | bytes 3227648 | tf_op jit(solution)/shard_map/qgjk,kgd->qgjd/dot_general | solution.py:32
  89.9 19.6 %while.72 = (s32[]{:T(128)}, f32[256,1,8]{0,2,1:T(8,128)S(1)}, f32[256,1,8]{0,2,1:T(8,128)S(1)}, f32[256,1,8,128]{0,3,2,1:T(8,128)S(1)}, s32[256]{0:T(256)}, /*i...) while((s32[]{:T(128)}, f32[256,1,8]{0,2,1:T(8,128)S(1)}, ...), condition=%wide.region_5.6_spmd.clone, body=%wide.region_2.5_spmd.clone.sunk | while | flops 272833024 | bytes 9314543 | solution.py:96
  113.4 2.5 %fusion.83 = f32[256,1,8,128]{3,0,2,1:T(8,128)} fusion(f32[256,1,8,256]{0,3,2,1:T(8,128)S(1)} %get-tuple-element.1192, f32[256,8]{0,1:T(8,128)S(1)} %get-tuple-element.1176, f32[256,8]{0,1:T(8,128)S(1)} %get-tuple-element.1174, bf16[1,1024,128]{2,1,0:T(8,128)(2,1)} %bitcast.434), kind=kOutput, calls=%fused_computation.122 | convolution fusion | flops 135528448 | bytes 3227648 | tf_op jit(solution)/shard_map/qgjk,kgd->qgjd/dot_general | solution.py:32
  117.5 19.7 %while.73 = (s32[]{:T(128)}, f32[256,1,8]{0,2,1:T(8,128)S(1)}, f32[256,1,8]{0,2,1:T(8,128)S(1)}, f32[256,1,8,128]{0,3,2,1:T(8,128)S(1)}, s32[256]{0:T(256)}, /*i...) while((s32[]{:T(128)}, f32[256,1,8]{0,2,1:T(8,128)S(1)}, ...), condition=%wide.region_11.12_spmd.clone, body=%wide.region_8.11_spmd.clone.sunk | while | flops 272833024 | bytes 9314543 | solution.py:96
  140.3 2.5 %fusion.85 = f32[256,1,8,128]{3,0,2,1:T(8,128)} fusion(f32[256,1,8,256]{0,3,2,1:T(8,128)S(1)} %get-tuple-element.1190, f32[256,8]{0,1:T(8,128)S(1)} %get-tuple-element.1179, f32[256,8]{0,1:T(8,128)S(1)} %get-tuple-element.1177, bf16[1,1024,128]{2,1,0:T(8,128)(2,1)} %bitcast.435), kind=kOutput, calls=%fused_computation.124 | convolution fusion | flops 135528448 | bytes 3227648 | tf_op jit(solution)/shard_map/qgjk,kgd->qgjd/dot_general | solution.py:32
  142.8 1.6 copy.75
  144.5 16.4 %while.74 = (s32[]{:T(128)}, f32[256,1,8]{0,2,1:T(8,128)S(1)}, f32[256,1,8]{0,2,1:T(8,128)S(1)}, f32[256,1,8,128]{0,3,2,1:T(8,128)S(1)}, s32[256]{0:T(256)S(1)},...) while((s32[]{:T(128)}, f32[256,1,8]{0,2,1:T(8,128)S(1)}, ...), condition=%wide.region_17.18_spmd.clone, body=%wide.region_14.17_spmd.clone.sunk | while | flops 272833024 | bytes 9314543 | solution.py:96
  163.9 2.5 %fusion.87 = f32[256,1,8,128]{3,0,2,1:T(8,128)} fusion(f32[256,1,8,256]{0,3,2,1:T(8,128)S(1)} %get-tuple-element.1188, f32[256,8]{0,1:T(8,128)S(1)} %get-tuple-element.1182, f32[256,8]{0,1:T(8,128)S(1)} %get-tuple-element.1180, bf16[1,1024,128]{2,1,0:T(8,128)(2,1)} %bitcast.436), kind=kOutput, calls=%fused_computation.126 | convolution fusion | flops 135528448 | bytes 3227648 | tf_op jit(solution)/shard_map/qgjk,kgd->qgjd/dot_general | solution.py:32
  168.1 16.6 %while.75 = (s32[]{:T(128)}, f32[256,1,8]{0,2,1:T(8,128)S(1)}, f32[256,1,8]{0,2,1:T(8,128)S(1)}, f32[256,1,8,128]{0,3,2,1:T(8,128)S(1)}, s32[256]{0:T(256)S(1)},...) while((s32[]{:T(128)}, f32[256,1,8]{0,2,1:T(8,128)S(1)}, ...), condition=%wide.region_23.24_spmd.clone, body=%wide.region_20.23_spmd.clone.sunk | while | flops 272833024 | bytes 9314543 | solution.py:96
  187.1 29.6 %all_to_all.67 = bf16[8,128,1024]{2,1,0:T(8,128)(2,1)S(1)} all-to-all(bf16[8,128,1024]{2,1,0:T(8,128)(2,1)S(1)} %bitcast.406), channel_id=1, replica_groups=mesh['ctx'=64,'head'=8] {'head'}, dimensions={0} | all-to-all | bytes 4194304 | tf_op jit(solution)/shard_map/all_to_all | solution.py:102
  216.8 2.4 %copy.85 = bf16[128,8,1024]{0,2,1:T(8,128)(2,1)} copy(bf16[128,8,1024]{2,0,1:T(8,128)(2,1)S(1)} %bitcast.407) | data formatting | bytes 4194304 | tf_op jit(solution)/shard_map/all_to_all | solution.py:102
  219.1 4.1 %copy.86 = bf16[128,8192]{1,0:T(8,128)(2,1)} copy(bf16[128,8192]{0,1:T(8,128)(2,1)} %bitcast.408) | data formatting | bytes 4194304 | tf_op jit(solution)/shard_map/all_to_all | solution.py:102
  (262 shorter events, 96.3 us)
Async XLA Ops:
  0.0 1.0 copy-start
  0.0 18.5 %copy-start.2 = (bf16[128,8192]{1,0:T(8,128)(2,1)S(1)}, bf16[128,8192]{1,0:T(8,128)(2,1)}, u32[]{:S(2)}) copy-start(bf16[128,8192]{1,0:T(8,128)(2,1)} %param.12) | copy-start | bytes 6291460
  1.7 13.4 %all-to-all-start = ((bf16[128,8,128]{2,0,1:T(8,128)(2,1)}), bf16[128,8,128]{2,0,1:T(8,128)(2,1)S(1)}, u32[]{:S(2)}, u32[]{:S(2)}) async-start(bf16[128,8,128]{2,0,1:T(8,128)(2,1)} %copy_bitcast_fusion.2), calls=%async_computation | async-start | bytes 524288 | tf_op jit(solution)/shard_map/all_to_all | solution.py:54
  15.1 10.6 %all-to-all-start.2 = ((bf16[128,8,128]{2,0,1:T(8,128)(2,1)}), bf16[128,8,128]{2,0,1:T(8,128)(2,1)S(1)}, u32[]{:S(2)}, u32[]{:S(2)}) async-start(bf16[128,8,128]{2,0,1:T(8,128)(2,1)} %copy_bitcast_fusion.1), calls=%async_computation.2 | async-start | bytes 524288 | tf_op jit(solution)/shard_map/all_to_all | solution.py:55
  25.7 43.3 %copy-start.1 = (bf16[128,8,128]{2,0,1:T(8,128)(2,1)}, bf16[128,8,128]{2,0,1:T(8,128)(2,1)S(1)}, u32[]{:S(2)}) copy-start(bf16[128,8,128]{2,0,1:T(8,128)(2,1)S(1)} %all-to-all-done.2) | copy-start | bytes 786436
  25.7 3.8 %copy-start.5 = (s32[65536]{0:T(1024)S(1)}, s32[65536]{0:T(1024)}, u32[]{:S(2)}) copy-start(s32[65536]{0:T(1024)} %param.15) | copy-start | bytes 786436
  25.7 57.9 %all-to-all-start.1 = ((bf16[128,8,1024]{2,0,1:T(8,128)(2,1)}), bf16[128,8,1024]{2,0,1:T(8,128)(2,1)S(1)}, u32[]{:S(2)}, u32[]{:S(2)}) async-start(bf16[128,8,1024]{2,0,1:T(8,128)(2,1)} %bitcast.405), calls=%async_computation.1 | async-start | bytes 4194304 | tf_op jit(solution)/shard_map/all_to_all | solution.py:53
  30.3 34.9 %copy-start.11 = (s32[256]{0:T(256)}, s32[256]{0:T(256)S(1)}, u32[]{:S(2)}) copy-start(s32[256]{0:T(256)S(1)} %get-tuple-element.1615) | copy-start | bytes 3076
  30.3 34.9 %copy-start.12 = (s32[256]{0:T(256)}, s32[256]{0:T(256)S(1)}, u32[]{:S(2)}) copy-start(s32[256]{0:T(256)S(1)} %get-tuple-element.1663) | copy-start | bytes 3076
  30.3 38.8 %copy-start.7 = (s32[256]{0:T(256)}, s32[256]{0:T(256)S(1)}, u32[]{:S(2)}) copy-start(s32[256]{0:T(256)S(1)} %get-tuple-element.1519) | copy-start | bytes 3076
  30.3 38.8 %copy-start.9 = (s32[256]{0:T(256)}, s32[256]{0:T(256)S(1)}, u32[]{:S(2)}) copy-start(s32[256]{0:T(256)S(1)} %get-tuple-element.1567) | copy-start | bytes 3076
  30.4 34.8 %collective-permute-start = (bf16[2,1024,128]{2,1,0:T(8,128)(2,1)S(1)}, bf16[2,1024,128]{2,1,0:T(8,128)(2,1)S(1)}, u32[]{:S(2)}, u32[]{:S(2)}) collective-permute-start(bf16[2,1024,128]{2,1,0:T(8,128)(2,1)S(1)} %pad_maximum_fusion.1), channel_id=1, source_target_pairs={{0,16},{8,24},{16,32},{24,40},{32,48},{40,56},{48,64},{56,72},{64,... | collective-permute-start | bytes 1572872 | tf_op jit(solution)/shard_map/ppermute | solution.py:19
  33.9 35.1 %collective-permute-start.1 = (bf16[2,1024,128]{2,1,0:T(8,128)(2,1)S(1)}, bf16[2,1024,128]{2,1,0:T(8,128)(2,1)S(1)}, u32[]{:S(2)}, u32[]{:S(2)}) collective-permute-start(bf16[2,1024,128]{2,1,0:T(8,128)(2,1)S(1)} %pad_maximum_fusion.1), channel_id=1, source_target_pairs={{0,8},{8,16},{16,24},{24,32},{32,40},{40,48},{48,56},{56,64},{64,7... | collective-permute-start | bytes 1572872 | tf_op jit(solution)/shard_map/ppermute | solution.py:19
  83.7 1.3 copy-start.6
  142.8 1.7 copy-start.10
  166.4 1.7 copy-start.8
  184.7 1.0 copy-start.3
  184.7 1.2 copy-start.4
where the time goes:
time: 226 us; the launch traced here: 223 us
  waiting for transfers between devices  55.2 us (24%)
  matrix products  52.6 us (23%)
  local copies, waits for them, and re-layouts  45.3 us (20%)
  blocking collectives  29.6 us (13%)
  other arithmetic  19.5 us (9%)
  starting transfers between devices  18.7 us (8%)
    ppermute x2, waiting for transfers between devices, from_behind(): lax.ppermute(value, axis, [(source, source + steps) for source in range(l...  32.1 us
    all_to_all x1, blocking collectives, shards(): lax.all_to_all(local_out, 'head', split_axis=0, concat_axis=1, tiled=True)  29.6 us
    dot_general x24, matrix products, attend_tile(): jnp.einsum('qgjd,kgd->qgjk', query_block, key_tile, preferred_element_typ...  28.9 us
    dot_general x24, matrix products, attend_tile(): jnp.einsum('qgjk,kgd->qgjd', weights.astype(jnp.bfloat16), value_tile, pr...  23.6 us
    dynamic_slice x21, local copies, waits for them, and re-layouts, visit(): tile_ids = lax.dynamic_slice_in_dim(window_ids, start, BLOCK)  15.2 us
    unnamed x39, local copies, waits for them, and re-layouts  13.2 us
    all_to_all x1, waiting for transfers between devices, shards(): lax.all_to_all(queries, 'head', split_axis=1, concat_axis=0, tiled=True)  11.9 us
    and x22, other arithmetic, visit(): (block_ids[:, None] == tile_ids[None, :]) & (key_pos[None, :] <= query_po...  10.1 us
  transfers between devices with their start and end apart: 5, of which 5 were waited for; matrix products, arithmetic and copies ran while one was open for 4% of the time, Pallas kernels for 0%

commit v1 on v0

--- a/solution.py
+++ b/solution.py
@@ -11,6 +11,13 @@
 QBLK_DEV = 4
 PREV = 2
 floor_score = -1e30
+
+
+def trade_parts(x, name, split, join):
+    peers = lax.axis_size(name)
+    parts = jnp.stack(jnp.split(x, peers, axis=split), axis=0)
+    parts = lax.all_to_all(parts, name, split_axis=0, concat_axis=0)
+    return jnp.concatenate(parts, axis=join)
 
 
 def from_behind(value, axis, steps):
@@ -52,7 +59,7 @@
     local_queries, local_keys, local_values = (
         lax.all_to_all(queries, "head", split_axis=1, concat_axis=0, tiled=True),
         lax.all_to_all(keys, "head", split_axis=1, concat_axis=0, tiled=True),
-        lax.all_to_all(values, "head", split_axis=1, concat_axis=0, tiled=True),
+        trade_parts(values, "head", 1, 0),
     )
     window = key_window(jnp.stack([local_keys, local_values]))
     groups = local_keys.shape[1] // HD

time: 226 us -> 198 us (0.88)
  local copies, waits for them, and re-layouts: 45.3 us -> 34.4 us
  matrix products: 52.6 us -> 44 us
  other arithmetic: 19.5 us -> 13.3 us
  waiting for transfers between devices: 55.2 us -> 50.8 us
  starting transfers between devices: 18.7 us -> 21 us
    dynamic_slice x21, local copies, waits for them, and re-layouts: 15.2 us -> 1.65 us  [visit(): tile_ids = lax.dynamic_slice_in_dim(window_ids, start, BLOCK)]
    dot_general x24, matrix products: 23.6 us -> 15.8 us  [attend_tile(): jnp.einsum('qgjk,kgd->qgjd', weights.astype(jnp.bfloat16), value_tile, pr...]
    and x22, other arithmetic: 10.1 us -> 3.84 us  [visit(): (block_ids[:, None] == tile_ids[None, :]) & (key_pos[None, :] <= query_po...]
    all_to_all x1, waiting for transfers between devices: 5.59 us -> 0.01 us  [shards(): lax.all_to_all(keys, 'head', split_axis=1, concat_axis=0, tiled=True)]
    unnamed x39 -> x46, local copies, waits for them, and re-layouts: 13.2 us -> 16.9 us
    all_to_all x1, starting transfers between devices: 3.41 us -> 5.7 us  [trade_parts(): parts = lax.all_to_all(parts, name, split_axis=0, concat_axis=0)]
  transfers between devices with their start and end apart: 5 -> 5, of which waited for: 5 -> 4; matrix products, arithmetic and copies ran while one was open for 4% -> 8% of each run, Pallas kernels for 0% -> 0%
where the time goes in v1:
time: 198 us; the launch traced here: 196 us
  waiting for transfers between devices  50.8 us (26%)
  matrix products  44 us (22%)
  local copies, waits for them, and re-layouts  34.4 us (17%)
  blocking collectives  30.4 us (15%)
  starting transfers between devices  21 us (11%)
  other arithmetic  13.3 us (7%)
    ppermute x2, waiting for transfers between devices, from_behind(): lax.ppermute(value, axis, [(source, source + steps) for source in range(l...  32.7 us
    all_to_all x1, blocking collectives, shards(): lax.all_to_all(local_out, 'head', split_axis=0, concat_axis=1, tiled=True)  30.4 us
    dot_general x24, matrix products, attend_tile(): jnp.einsum('qgjd,kgd->qgjk', query_block, key_tile, preferred_element_typ...  28.1 us
    unnamed x46, local copies, waits for them, and re-layouts  16.9 us
    dot_general x24, matrix products, attend_tile(): jnp.einsum('qgjk,kgd->qgjd', weights.astype(jnp.bfloat16), value_tile, pr...  15.8 us
    all_to_all x1, waiting for transfers between devices, shards(): lax.all_to_all(queries, 'head', split_axis=1, concat_axis=0, tiled=True)  12.4 us
    reduce_sum x24, other arithmetic, attend_tile(): totals = totals * factor + jnp.sum(weights, axis=-1)  7.06 us
    all_to_all x2, local copies, waits for them, and re-layouts, shards(): lax.all_to_all(local_out, 'head', split_axis=0, concat_axis=1, tiled=True)  6.44 us
  transfers between devices with their start and end apart: 5, of which 4 were waited for; matrix products, arithmetic and copies ran while one was open for 8% of the time, Pallas kernels for 0%

profile of v1, /device:TPU:128, one launch (start us, length us, event | category | flops | bytes accessed | tf_op | source)
XLA Modules:
  0.0 195.8 jit_solution(15105151583968908754)
XLA Ops:
  1.7 6.1 %all-to-all-start = ((bf16[128,8,128]{2,0,1:T(8,128)(2,1)}), bf16[128,8,128]{2,0,1:T(8,128)(2,1)S(1)}, u32[]{:S(2)}, u32[]{:S(2)}) async-start(bf16[128,8,128]{2,0,1:T(8,128)(2,1)} %copy_bitcast_fusion.1), calls=%async_computation | async-start | bytes 524288 | tf_op jit(solution)/shard_map/all_to_all | solution.py:61
  7.8 1.4 bitcast_dynamic-update-slice_fusion.7
  10.5 1.4 bitcast_dynamic-update-slice_fusion.5
  11.9 1.4 bitcast_dynamic-update-slice_fusion.4
  13.3 1.4 bitcast_dynamic-update-slice_fusion.3
  16.0 1.4 bitcast_dynamic-update-slice_fusion.1
  17.3 1.4 bitcast_dynamic-update-slice_fusion
  18.7 5.7 %all-to-all-start.2 = ((bf16[8,128,128]{2,1,0:T(8,128)(2,1)}), bf16[8,128,128]{2,1,0:T(8,128)(2,1)S(1)}, u32[]{:S(2)}, u32[]{:S(2)}) async-start(bf16[8,128,128]{2,1,0:T(8,128)(2,1)} %bitcast_dynamic-update-slice_fusion), calls=%async_computation.2 | async-start | bytes 524288 | tf_op jit(solution)/shard_map/all_to_all | solution.py:19
  24.4 1.6 copy.132
  26.0 5.7 %all-to-all-done.2 = bf16[8,128,128]{2,1,0:T(8,128)(2,1)S(1)} async-done(((bf16[8,128,128]{2,1,0:T(8,128)(2,1)}), bf16[8,128,128]{2,1,0:T(8,128)(2,1)S(1)}, u32[]{:S(2)}, u32[]{:S(2)}) %all-to-all-start.2) | async-done | bytes 262176 | tf_op jit(solution)/shard_map/all_to_all | solution.py:19
  31.7 3.7 %all-to-all-start.1 = ((bf16[128,8,1024]{2,0,1:T(8,128)(2,1)}), bf16[128,8,1024]{2,0,1:T(8,128)(2,1)S(1)}, u32[]{:S(2)}, u32[]{:S(2)}) async-start(bf16[128,8,1024]{2,0,1:T(8,128)(2,1)} %bitcast.410), calls=%async_computation.1 | async-start | bytes 4194304 | tf_op jit(solution)/shard_map/all_to_all | solution.py:60
  35.8 3.5 %collective-permute-start = (bf16[2,1024,128]{2,1,0:T(8,128)(2,1)S(1)}, bf16[2,1024,128]{2,1,0:T(8,128)(2,1)S(1)}, u32[]{:S(2)}, u32[]{:S(2)}) collective-permute-start(bf16[2,1024,128]{2,1,0:T(8,128)(2,1)S(1)} %pad_maximum_fusion.1), channel_id=1, source_target_pairs={{0,16},{8,24},{16,32},{24,40},{32,48},{40,56},{48,64},{56,72},{64,... | collective-permute-start | bytes 1572872 | tf_op jit(solution)/shard_map/ppermute | solution.py:26
  39.3 1.9 collective-permute-start.1
  42.3 28.1 %collective-permute-done = bf16[2,1024,128]{2,1,0:T(8,128)(2,1)S(1)} collective-permute-done((bf16[2,1024,128]{2,1,0:T(8,128)(2,1)S(1)}, bf16[2,1024,128]{2,1,0:T(8,128)(2,1)S(1)}, u32[]{:S(2)}, u32[]{:S(2)}) %collective-permute-start) | collective-permute-done | bytes 524320 | tf_op jit(solution)/shard_map/ppermute | solution.py:26
  70.4 4.6 %collective-permute-done.1 = bf16[2,1024,128]{2,1,0:T(8,128)(2,1)S(1)} collective-permute-done((bf16[2,1024,128]{2,1,0:T(8,128)(2,1)S(1)}, bf16[2,1024,128]{2,1,0:T(8,128)(2,1)S(1)}, u32[]{:S(2)}, u32[]{:S(2)}) %collective-permute-start.1) | collective-permute-done | bytes 524320 | tf_op jit(solution)/shard_map/ppermute | solution.py:26
  76.4 1.4 copy.62
  77.8 12.4 %all-to-all-done.1 = bf16[128,8,1024]{2,0,1:T(8,128)(2,1)S(1)} async-done(((bf16[128,8,1024]{2,0,1:T(8,128)(2,1)}), bf16[128,8,1024]{2,0,1:T(8,128)(2,1)S(1)}, u32[]{:S(2)}, u32[]{:S(2)}) %all-to-all-start.1) | async-done | bytes 2097184 | tf_op jit(solution)/shard_map/all_to_all | solution.py:60
  93.1 13.2 %while.72 = (s32[]{:T(128)}, f32[256,1,8]{0,2,1:T(8,128)S(1)}, f32[256,1,8]{0,2,1:T(8,128)S(1)}, f32[256,1,8,128]{0,3,2,1:T(8,128)S(1)}, s32[256]{0:T(256)S(1)},...) while((s32[]{:T(128)}, f32[256,1,8]{0,2,1:T(8,128)S(1)}, ...), condition=%wide.region_5.6_spmd.clone, body=%wide.region_2.5_spmd.clone.sunk | while | flops 272833024 | bytes 9314543 | solution.py:103
  110.1 13.0 %while.73 = (s32[]{:T(128)}, f32[256,1,8]{0,2,1:T(8,128)S(1)}, f32[256,1,8]{0,2,1:T(8,128)S(1)}, f32[256,1,8,128]{0,3,2,1:T(8,128)S(1)}, s32[256]{0:T(256)S(1)},...) while((s32[]{:T(128)}, f32[256,1,8]{0,2,1:T(8,128)S(1)}, ...), condition=%wide.region_11.12_spmd.clone, body=%wide.region_8.11_spmd.clone.sunk | while | flops 272833024 | bytes 9314543 | solution.py:103
  126.8 13.0 %while.74 = (s32[]{:T(128)}, f32[256,1,8]{0,2,1:T(8,128)S(1)}, f32[256,1,8]{0,2,1:T(8,128)S(1)}, f32[256,1,8,128]{0,3,2,1:T(8,128)S(1)}, s32[256]{0:T(256)S(1)},...) while((s32[]{:T(128)}, f32[256,1,8]{0,2,1:T(8,128)S(1)}, ...), condition=%wide.region_17.18_spmd.clone, body=%wide.region_14.17_spmd.clone.sunk | while | flops 272833024 | bytes 9314543 | solution.py:103
  143.5 13.0 %while.75 = (s32[]{:T(128)}, f32[256,1,8]{0,2,1:T(8,128)S(1)}, f32[256,1,8]{0,2,1:T(8,128)S(1)}, f32[256,1,8,128]{0,3,2,1:T(8,128)S(1)}, s32[256]{0:T(256)S(1)},...) while((s32[]{:T(128)}, f32[256,1,8]{0,2,1:T(8,128)S(1)}, ...), condition=%wide.region_23.24_spmd.clone, body=%wide.region_20.23_spmd.clone.sunk | while | flops 272833024 | bytes 9314543 | solution.py:103
  159.0 30.4 %all_to_all.56 = bf16[8,128,1024]{2,1,0:T(8,128)(2,1)S(1)} all-to-all(bf16[8,128,1024]{2,1,0:T(8,128)(2,1)S(1)} %bitcast.411), channel_id=1, replica_groups=mesh['ctx'=64,'head'=8] {'head'}, dimensions={0} | all-to-all | bytes 4194304 | tf_op jit(solution)/shard_map/all_to_all | solution.py:109
  189.4 2.4 %copy.82 = bf16[128,8,1024]{0,2,1:T(8,128)(2,1)} copy(bf16[128,8,1024]{2,0,1:T(8,128)(2,1)S(1)} %bitcast.412) | data formatting | bytes 4194304 | tf_op jit(solution)/shard_map/all_to_all | solution.py:109
  191.8 4.1 %copy.83 = bf16[128,8192]{1,0:T(8,128)(2,1)} copy(bf16[128,8192]{0,1:T(8,128)(2,1)} %bitcast.413) | data formatting | bytes 4194304 | tf_op jit(solution)/shard_map/all_to_all | solution.py:109
  (269 shorter events, 74.0 us)
Async XLA Ops:
  0.0 1.0 copy-start
  0.0 24.4 %copy-start.3 = (bf16[128,8192]{1,0:T(8,128)(2,1)S(1)}, bf16[128,8192]{1,0:T(8,128)(2,1)}, u32[]{:S(2)}) copy-start(bf16[128,8192]{1,0:T(8,128)(2,1)} %param.12) | copy-start | bytes 6291460
  1.7 17.0 %all-to-all-start = ((bf16[128,8,128]{2,0,1:T(8,128)(2,1)}), bf16[128,8,128]{2,0,1:T(8,128)(2,1)S(1)}, u32[]{:S(2)}, u32[]{:S(2)}) async-start(bf16[128,8,128]{2,0,1:T(8,128)(2,1)} %copy_bitcast_fusion.1), calls=%async_computation | async-start | bytes 524288 | tf_op jit(solution)/shard_map/all_to_all | solution.py:61
  18.7 13.0 %all-to-all-start.2 = ((bf16[8,128,128]{2,1,0:T(8,128)(2,1)}), bf16[8,128,128]{2,1,0:T(8,128)(2,1)S(1)}, u32[]{:S(2)}, u32[]{:S(2)}) async-start(bf16[8,128,128]{2,1,0:T(8,128)(2,1)} %bitcast_dynamic-update-slice_fusion), calls=%async_computation.2 | async-start | bytes 524288 | tf_op jit(solution)/shard_map/all_to_all | solution.py:19
  31.7 43.3 %copy-start.1 = (bf16[8,128,128]{2,1,0:T(8,128)(2,1)}, bf16[8,128,128]{2,1,0:T(8,128)(2,1)S(1)}, u32[]{:S(2)}) copy-start(bf16[8,128,128]{2,1,0:T(8,128)(2,1)S(1)} %all-to-all-done.2) | copy-start | bytes 786436
  31.7 3.8 %copy-start.6 = (s32[65536]{0:T(1024)S(1)}, s32[65536]{0:T(1024)}, u32[]{:S(2)}) copy-start(s32[65536]{0:T(1024)} %param.15) | copy-start | bytes 786436
  31.7 58.5 %all-to-all-start.1 = ((bf16[128,8,1024]{2,0,1:T(8,128)(2,1)}), bf16[128,8,1024]{2,0,1:T(8,128)(2,1)S(1)}, u32[]{:S(2)}, u32[]{:S(2)}) async-start(bf16[128,8,1024]{2,0,1:T(8,128)(2,1)} %bitcast.410), calls=%async_computation.1 | async-start | bytes 4194304 | tf_op jit(solution)/shard_map/all_to_all | solution.py:60
  35.7 6.4 %copy-start.11 = (s32[256]{0:T(256)}, s32[256]{0:T(256)S(1)}, u32[]{:S(2)}) copy-start(s32[256]{0:T(256)S(1)} %get-tuple-element.1615) | copy-start | bytes 3076
  35.7 6.4 %copy-start.13 = (s32[256]{0:T(256)}, s32[256]{0:T(256)S(1)}, u32[]{:S(2)}) copy-start(s32[256]{0:T(256)S(1)} %get-tuple-element.1663) | copy-start | bytes 3076
  35.7 34.7 %copy-start.9 = (s32[256]{0:T(256)}, s32[256]{0:T(256)S(1)}, u32[]{:S(2)}) copy-start(s32[256]{0:T(256)S(1)} %get-tuple-element.1567) | copy-start | bytes 3076
  35.8 34.6 %collective-permute-start = (bf16[2,1024,128]{2,1,0:T(8,128)(2,1)S(1)}, bf16[2,1024,128]{2,1,0:T(8,128)(2,1)S(1)}, u32[]{:S(2)}, u32[]{:S(2)}) collective-permute-start(bf16[2,1024,128]{2,1,0:T(8,128)(2,1)S(1)} %pad_maximum_fusion.1), channel_id=1, source_target_pairs={{0,16},{8,24},{16,32},{24,40},{32,48},{40,56},{48,64},{56,72},{64,... | collective-permute-start | bytes 1572872 | tf_op jit(solution)/shard_map/ppermute | solution.py:26
  39.3 35.7 %collective-permute-start.1 = (bf16[2,1024,128]{2,1,0:T(8,128)(2,1)S(1)}, bf16[2,1024,128]{2,1,0:T(8,128)(2,1)S(1)}, u32[]{:S(2)}, u32[]{:S(2)}) collective-permute-start(bf16[2,1024,128]{2,1,0:T(8,128)(2,1)S(1)} %pad_maximum_fusion.1), channel_id=1, source_target_pairs={{0,8},{8,16},{16,24},{24,32},{32,40},{40,48},{48,56},{56,64},{64,7... | collective-permute-start | bytes 1572872 | tf_op jit(solution)/shard_map/ppermute | solution.py:26
  90.2 1.3 copy-start.8
  91.5 1.0 copy-start.2
  92.4 0.7 copy-start.14
  106.3 2.3 %copy-start.7 = (pred[256,256]{0,1:T(8,128)(4,1)S(1)}, pred[256,256]{0,1:T(8,128)(4,1)}, u32[]{:S(2)}) copy-start(pred[256,256]{0,1:T(8,128)(4,1)} %get-tuple-element.1197) | copy-start | bytes 196612
  109.4 0.7 copy-start.12
  126.1 0.7 copy-start.10
  156.5 1.0 copy-start.4
  156.6 1.2 copy-start.5
